TPU v7x, 32 devices: a whole 2x2x4 slice. The times are simulated.
32 devices in a mesh: ev: 8 (over z, y), col: 4 (over x, core).
Axes of the slice: x: 2, y: 2, z: 4, core: 2. Of those that a mesh axis runs over, the one named last changes fastest.
Arguments:
- panel: bfloat16 [256, 131072], P('col', 'ev'), may hold values from -12 to 12
- signs: int32 [131072], P('ev'), may hold values from -1 to 1, as said below
- offsets: int32 [2048], replicated, may hold values from 0 to 63
Outputs:
- gram: float32 [256, 256], P('col')
Inputs may be any that keep to these rules, and one draw needn't show every extreme that they name: `signs`: every entry is -1 or +1.
All inputs are finite; a program needn't handle non-finite values.
Results may differ from a plain program's by a relative error of at most 0.0003.
Values sent between devices are 32-bit elements; how exact they have to be, the bound alone decides.
No kernel may reach another device: no remote copies, remote signals or barrier semaphores. Data moves between devices by JAX's collectives and lax.ppermute only.
A program may use at most 64 MiB of HBM per device.

v0:
```python
import math
import jax
import jax.numpy as jnp
from jax import lax
from jax.sharding import PartitionSpec as P

STRIDE = 64


def swapped(value, axis, stride):
    mask = 2**stride
    pairs = [(source, source ^ mask) for source in range(lax.axis_size(axis))]
    return lax.ppermute(value, axis, pairs)


def hadamard(order):
    index = jnp.arange(order, dtype=jnp.int32)
    both = index[:, None] & index[None, :]
    parity = jnp.zeros((order, order), jnp.int32)
    for level in range(order.bit_length() - 1):
        parity = parity + (both >> level & 1)
    return (1 - 2 * (parity % 2)).astype(jnp.float32)


def pick_local(values, offsets, my_index, strata):
    columns = values.shape[0]
    chosen = lax.dynamic_slice_in_dim(offsets, my_index * strata, strata)
    grouped = values.reshape(columns, strata, STRIDE)
    return jnp.take_along_axis(grouped, chosen[None, :, None], axis=2)[:, :, 0]


def per_device(panel, signs, offsets):
    columns, length = panel.shape
    groups = lax.axis_size("ev")
    my_index = lax.axis_index("ev")
    inner_len = length // 128
    strata = length // STRIDE
    high = lax.Precision.HIGHEST
    signed = panel * signs.astype(jnp.bfloat16)[None, :]
    blocks = signed.reshape(columns, 128, inner_len)
    first = jnp.einsum(
        "xa,cab->cxb",
        hadamard(128).astype(jnp.bfloat16),
        blocks,
        preferred_element_type=jnp.float32,
    )
    local = jnp.einsum("yb,cxb->cxy", hadamard(inner_len), first, precision=high).reshape(
        columns, length
    )
    total_events = length * groups
    scale = 1.0 / math.sqrt(total_events * (total_events // STRIDE))
    values = local
    for level in range(groups.bit_length() - 1):
        partner = swapped(values, "ev", level)
        upper_half = my_index >> level & 1 == 1
        values = jnp.where(upper_half, partner - values, values + partner)
    picked = pick_local(values, offsets, my_index, strata)
    sketch = picked * scale
    partial_gram = jnp.dot(
        sketch,
        lax.all_gather(sketch, "col", axis=0, tiled=True).T,
        precision=high,
        preferred_element_type=jnp.float32,
    )
    return lax.psum(partial_gram, "ev")


def solution(mesh):
    return jax.shard_map(
        per_device,
        mesh=mesh,
        in_specs=(P("col", "ev"), P("ev"), P()),
        out_specs=P("col", None),
        check_vma=False,
    )
```

profile of v0, /device:TPU:0, one launch (start us, length us, event | category | flops | bytes accessed | tf_op | source)
XLA Modules:
  0.0 503.6 jit_solution(14643924601332694307)
XLA Ops:
  6.5 0.0 all-reduce.2.cloned.1.call-start
  6.5 0.8 convert_element_type.12
  7.4 1.9 multiply_bitcast_fusion
  9.2 0.6 copy.12
  9.8 0.8 fusion.12
  10.6 6.7 %fusion = f32[64,128,128]{2,1,0:T(8,128)S(1)} fusion(f32[64,128,128]{2,1,0:T(8,128)S(1)} %fusion.12), kind=kOutput, calls=%fused_computation.2 | convolution fusion | flops 1611186176 | bytes 8388608 | tf_op jit(solution)/shard_map/yb,cxb->cxy/dot_general | solution.py:47
  17.3 0.0 copy-start
  17.3 4.3 copy.17
  21.6 0.0 copy-done
  21.6 3.0 collective-permute-start
  24.6 90.9 %collective-permute-done = f32[64,16384]{1,0:T(8,128)} collective-permute-done((f32[64,16384]{1,0:T(8,128)}, f32[64,16384]{1,0:T(8,128)}, u32[]{:S(2)}, u32[]{:S(2)}) %collective-permute-start) | collective-permute-done | bytes 4194336 | tf_op jit(solution)/shard_map/ppermute | solution.py:13
  115.5 8.4 %add_select_fusion.2 = f32[64,16384]{1,0:T(8,128)} fusion(f32[64,16384]{1,0:T(8,128)} %collective-permute-done, pred[]{:T(512)S(6)} %eq.14, f32[8,8,128,128]{3,2,1,0:T(8,128)} %bitcast.28), kind=kLoop, calls=%fused_computation.6 | loop fusion | flops 3145728 | bytes 12582913 | tf_op jit(solution)/shard_map/jit(_where)/select_n | solution.py:56
  123.9 1.8 collective-permute-start.1
  125.7 90.3 %collective-permute-done.1 = f32[64,16384]{1,0:T(8,128)} collective-permute-done((f32[64,16384]{1,0:T(8,128)}, f32[64,16384]{1,0:T(8,128)}, u32[]{:S(2)}, u32[]{:S(2)}) %collective-permute-start.1) | collective-permute-done | bytes 4194336 | tf_op jit(solution)/shard_map/ppermute | solution.py:13
  216.0 5.9 %add_select_fusion.1 = f32[64,16384]{1,0:T(8,128)} fusion(f32[64,16384]{1,0:T(8,128)} %add_select_fusion.2, f32[64,16384]{1,0:T(8,128)} %collective-permute-done.1, pred[]{:T(512)S(6)} %eq.13), kind=kLoop, calls=%fused_computation.5 | loop fusion | flops 3145728 | bytes 12582913 | tf_op jit(solution)/shard_map/jit(_where)/select_n | solution.py:56
  221.8 2.5 collective-permute-start.2
  224.3 0.8 compare_and_fusion
  225.1 178.6 %collective-permute-done.2 = f32[64,16384]{1,0:T(8,128)} collective-permute-done((f32[64,16384]{1,0:T(8,128)}, f32[64,16384]{1,0:T(8,128)}, u32[]{:S(2)}, u32[]{:S(2)}) %collective-permute-start.2) | collective-permute-done | bytes 4194336 | tf_op jit(solution)/shard_map/ppermute | solution.py:13
  403.8 5.9 %add_select_fusion = f32[64,16384]{1,0:T(8,128)} fusion(f32[64,16384]{1,0:T(8,128)} %add_select_fusion.1, f32[64,16384]{1,0:T(8,128)} %collective-permute-done.2, pred[]{:T(512)S(6)} %eq.12), kind=kLoop, calls=%fused_computation.4 | loop fusion | flops 3145728 | bytes 12582913 | tf_op jit(solution)/shard_map/jit(_where)/select_n | solution.py:56
  409.6 6.9 %copy.8 = f32[64,16384]{0,1:T(8,128)} copy(f32[64,16384]{1,0:T(8,128)} %add_select_fusion) | data formatting | bytes 8388608 | tf_op jit(solution)/shard_map/jit(_where)/select_n | solution.py:56
  416.5 2.3 gather_fusion
  418.9 0.1 fusion.3
  419.0 0.1 copy.9
  419.1 5.8 %all_gather.3 = f32[256,256]{1,0:T(8,128)S(1)} all-gather(f32[64,256]{1,0:T(8,128)S(1)} %copy.9), channel_id=1, replica_groups=mesh['ev'=8,'col'=4] {'col'}, dimensions={0}, use_global_device_ids=true | all-gather | bytes 327680 | tf_op jit(solution)/shard_map/all_gather | solution.py:61
  424.8 1.1 fusion.2
  425.9 0.0 all-reduce.2.cloned.1.call-update
  425.9 69.4 %all-reduce.2.cloned.1.call-done = f32[64,256]{1,0:T(8,128)} async-done(((f32[64,256]{1,0:T(8,128)}), f32[64,256]{1,0:T(8,128)}) %all-reduce.2.cloned.1.call-update) | async-done | bytes 65552 | tf_op jit(solution)/shard_map/psum | solution.py:65
  495.3 1.5 copy.19
  (3 shorter events, 0.0 us)
Async XLA Ops:
  6.5 488.8 %all-reduce.2.cloned.1.call-start = ((), (), s32[]{:S(2)}) async-start(), calls=%async_computation | async-start | bytes 131072 | tf_op jit(solution)/shard_map/psum | solution.py:65
  17.3 4.3 copy-start
  21.6 93.9 %collective-permute-start = (f32[64,16384]{1,0:T(8,128)}, f32[64,16384]{1,0:T(8,128)}, u32[]{:S(2)}, u32[]{:S(2)}) collective-permute-start(f32[64,16384]{1,0:T(8,128)} %bitcast.26), channel_id=1, source_target_pairs={{0,4},{4,0},{8,12},{12,8},{16,20},{20,16},{24,28},{28,24},{1,5},{5... | collective-permute-start | bytes 12582920 | tf_op jit(solution)/shard_map/ppermute | solution.py:13
  123.9 92.1 %collective-permute-start.1 = (f32[64,16384]{1,0:T(8,128)}, f32[64,16384]{1,0:T(8,128)}, u32[]{:S(2)}, u32[]{:S(2)}) collective-permute-start(f32[64,16384]{1,0:T(8,128)} %add_select_fusion.2), channel_id=1, source_target_pairs={{0,8},{4,12},{8,0},{12,4},{16,24},{20,28},{24,16},{28,20},{1,9},{5... | collective-permute-start | bytes 12582920 | tf_op jit(solution)/shard_map/ppermute | solution.py:13
  221.8 181.9 %collective-permute-start.2 = (f32[64,16384]{1,0:T(8,128)}, f32[64,16384]{1,0:T(8,128)}, u32[]{:S(2)}, u32[]{:S(2)}) collective-permute-start(f32[64,16384]{1,0:T(8,128)} %add_select_fusion.1), channel_id=1, source_target_pairs={{0,16},{4,20},{8,24},{12,28},{16,0},{20,4},{24,8},{28,12},{1,17},{... | collective-permute-start | bytes 12582920 | tf_op jit(solution)/shard_map/ppermute | solution.py:13
Sparse Core Ops, SparseCore 0:
  426.1 69.1 all-reduce.1
where the time goes:
time: 504 us
  waiting for transfers between devices  429 us (85%)
  other arithmetic  23.7 us (5%)
  local copies, waits for them, and re-layouts  15.7 us (3%)
  between operations  13.4 us (3%)
  matrix products  8.53 us (2%)
  starting transfers between devices  7.27 us (1%)
  blocking collectives  5.79 us (1%)
    ppermute x3, waiting for transfers between devices, swapped(): return lax.ppermute(value, axis, pairs)  360 us
    psum x1, waiting for transfers between devices, per_device(): return lax.psum(partial_gram, 'ev')  69.4 us
    select_n x3, other arithmetic, per_device(): values = jnp.where(upper_half, partner - values, values + partner)  20.1 us
  transfers between devices with their start and end apart: 4, of which 4 were waited for; matrix products, arithmetic and copies ran while one was open for 0% of the time, Pallas kernels for 0%

commit v1 on v0

--- a/solution.py
+++ b/solution.py
@@ -5,6 +5,11 @@
 from jax.sharding import PartitionSpec as P
 
 STRIDE = 64
+
+
+def summed_here(shard, mesh_axis):
+    parts = lax.all_gather(shard, mesh_axis)
+    return jnp.sum(parts, axis=0)
 
 
 def swapped(value, axis, stride):
@@ -62,7 +67,7 @@
         precision=high,
         preferred_element_type=jnp.float32,
     )
-    return lax.psum(partial_gram, "ev")
+    return summed_here(partial_gram, "ev")
 
 
 def solution(mesh):

time: 504 us -> 451 us (0.89)
  waiting for transfers between devices: 429 us -> 360 us
  blocking collectives: 5.79 us -> 37.2 us
  between operations: 13.4 us -> 0.07 us
    psum x1 -> x0, waiting for transfers between devices: 69.4 us -> none  [per_device(): return lax.psum(partial_gram, 'ev')]
    all_gather x0 -> x1, blocking collectives: none -> 31.4 us  [summed_here(): parts = lax.all_gather(shard, mesh_axis)]
  transfers between devices with their start and end apart: 4 -> 3, of which waited for: 4 -> 3; matrix products, arithmetic and copies ran while one was open for 0% -> 0% of each run, Pallas kernels for 0% -> 0%
where the time goes in v1:
time: 451 us
  waiting for transfers between devices  360 us (80%)
  blocking collectives  37.2 us (8%)
  other arithmetic  24.4 us (5%)
  local copies, waits for them, and re-layouts  14.2 us (3%)
  matrix products  8.1 us (2%)
  starting transfers between devices  7.26 us (2%)
    ppermute x3, waiting for transfers between devices, swapped(): return lax.ppermute(value, axis, pairs)  360 us
    all_gather x1, blocking collectives, summed_here(): parts = lax.all_gather(shard, mesh_axis)  31.4 us
    select_n x3, other arithmetic, per_device(): values = jnp.where(upper_half, partner - values, values + partner)  20.1 us
  transfers between devices with their start and end apart: 3, of which 3 were waited for; matrix products, arithmetic and copies ran while one was open for 0% of the time, Pallas kernels for 0%

profile of v1, /device:TPU:0, one launch (start us, length us, event | category | flops | bytes accessed | tf_op | source)
XLA Modules:
  0.0 451.0 jit_solution(9383943741397265987)
XLA Ops:
  0.0 0.8 convert_element_type.12
  0.8 1.9 multiply_bitcast_fusion
  2.7 0.6 copy.12
  3.3 0.8 fusion.12
  4.1 6.9 %fusion = f32[64,128,128]{2,1,0:T(8,128)S(1)} fusion(f32[64,128,128]{2,1,0:T(8,128)S(1)} %fusion.12), kind=kOutput, calls=%fused_computation.2 | convolution fusion | flops 1611186176 | bytes 8388608 | tf_op jit(solution)/shard_map/yb,cxb->cxy/dot_general | solution.py:52
  10.9 0.0 copy-start
  11.0 4.3 copy.17
  15.3 0.0 copy-done
  15.3 3.0 collective-permute-start
  18.3 90.9 %collective-permute-done = f32[64,16384]{1,0:T(8,128)} collective-permute-done((f32[64,16384]{1,0:T(8,128)}, f32[64,16384]{1,0:T(8,128)}, u32[]{:S(2)}, u32[]{:S(2)}) %collective-permute-start) | collective-permute-done | bytes 4194336 | tf_op jit(solution)/shard_map/ppermute | solution.py:18
  109.1 8.4 %add_select_fusion.2 = f32[64,16384]{1,0:T(8,128)} fusion(f32[64,16384]{1,0:T(8,128)} %collective-permute-done, pred[]{:T(512)S(6)} %eq.14, f32[8,8,128,128]{3,2,1,0:T(8,128)} %bitcast.29), kind=kLoop, calls=%fused_computation.6 | loop fusion | flops 3145728 | bytes 12582913 | tf_op jit(solution)/shard_map/jit(_where)/select_n | solution.py:61
  117.5 1.8 collective-permute-start.1
  119.3 90.3 %collective-permute-done.1 = f32[64,16384]{1,0:T(8,128)} collective-permute-done((f32[64,16384]{1,0:T(8,128)}, f32[64,16384]{1,0:T(8,128)}, u32[]{:S(2)}, u32[]{:S(2)}) %collective-permute-start.1) | collective-permute-done | bytes 4194336 | tf_op jit(solution)/shard_map/ppermute | solution.py:18
  209.6 5.9 %add_select_fusion.1 = f32[64,16384]{1,0:T(8,128)} fusion(f32[64,16384]{1,0:T(8,128)} %add_select_fusion.2, f32[64,16384]{1,0:T(8,128)} %collective-permute-done.1, pred[]{:T(512)S(6)} %eq.13), kind=kLoop, calls=%fused_computation.5 | loop fusion | flops 3145728 | bytes 12582913 | tf_op jit(solution)/shard_map/jit(_where)/select_n | solution.py:61
  215.5 2.5 collective-permute-start.2
  218.0 0.8 compare_and_fusion
  218.8 178.7 %collective-permute-done.2 = f32[64,16384]{1,0:T(8,128)} collective-permute-done((f32[64,16384]{1,0:T(8,128)}, f32[64,16384]{1,0:T(8,128)}, u32[]{:S(2)}, u32[]{:S(2)}) %collective-permute-start.2) | collective-permute-done | bytes 4194336 | tf_op jit(solution)/shard_map/ppermute | solution.py:18
  397.4 5.9 %add_select_fusion = f32[64,16384]{1,0:T(8,128)} fusion(f32[64,16384]{1,0:T(8,128)} %add_select_fusion.1, f32[64,16384]{1,0:T(8,128)} %collective-permute-done.2, pred[]{:T(512)S(6)} %eq.12), kind=kLoop, calls=%fused_computation.4 | loop fusion | flops 3145728 | bytes 12582913 | tf_op jit(solution)/shard_map/jit(_where)/select_n | solution.py:61
  403.3 6.9 %copy.8 = f32[64,16384]{0,1:T(8,128)} copy(f32[64,16384]{1,0:T(8,128)} %add_select_fusion) | data formatting | bytes 8388608 | tf_op jit(solution)/shard_map/jit(_where)/select_n | solution.py:61
  410.2 2.3 gather_fusion
  412.5 0.1 fusion.3
  412.6 0.1 copy.9
  412.7 5.8 %all_gather.9 = f32[256,256]{1,0:T(8,128)S(1)} all-gather(f32[64,256]{1,0:T(8,128)S(1)} %copy.9), channel_id=1, replica_groups=mesh['ev'=8,'col'=4] {'col'}, dimensions={0}, use_global_device_ids=true | all-gather | bytes 327680 | tf_op jit(solution)/shard_map/all_gather | solution.py:66
  418.5 0.4 fusion.2
  419.0 31.4 %all-gather = f32[512,256]{1,0:T(8,128)S(1)} all-gather(f32[64,256]{1,0:T(8,128)S(1)} %fusion.2), channel_id=2, replica_groups=mesh['ev'=8,'col'=4] {'ev'}, dimensions={0}, use_global_device_ids=true | all-gather | bytes 589824 | tf_op jit(solution)/shard_map/all_gather | solution.py:11
  450.3 0.7 reduce_sum.9
  (3 shorter events, 0.0 us)
Async XLA Ops:
  10.9 4.3 copy-start
  15.3 93.9 %collective-permute-start = (f32[64,16384]{1,0:T(8,128)}, f32[64,16384]{1,0:T(8,128)}, u32[]{:S(2)}, u32[]{:S(2)}) collective-permute-start(f32[64,16384]{1,0:T(8,128)} %bitcast.27), channel_id=1, source_target_pairs={{0,4},{4,0},{8,12},{12,8},{16,20},{20,16},{24,28},{28,24},{1,5},{5... | collective-permute-start | bytes 12582920 | tf_op jit(solution)/shard_map/ppermute | solution.py:18
  117.5 92.1 %collective-permute-start.1 = (f32[64,16384]{1,0:T(8,128)}, f32[64,16384]{1,0:T(8,128)}, u32[]{:S(2)}, u32[]{:S(2)}) collective-permute-start(f32[64,16384]{1,0:T(8,128)} %add_select_fusion.2), channel_id=1, source_target_pairs={{0,8},{4,12},{8,0},{12,4},{16,24},{20,28},{24,16},{28,20},{1,9},{5... | collective-permute-start | bytes 12582920 | tf_op jit(solution)/shard_map/ppermute | solution.py:18
  215.5 181.9 %collective-permute-start.2 = (f32[64,16384]{1,0:T(8,128)}, f32[64,16384]{1,0:T(8,128)}, u32[]{:S(2)}, u32[]{:S(2)}) collective-permute-start(f32[64,16384]{1,0:T(8,128)} %add_select_fusion.1), channel_id=1, source_target_pairs={{0,16},{4,20},{8,24},{12,28},{16,0},{20,4},{24,8},{28,12},{1,17},{... | collective-permute-start | bytes 12582920 | tf_op jit(solution)/shard_map/ppermute | solution.py:18
